TPU v7x, 32 devices: a whole 2x2x4 slice. The times are simulated.
32 devices in a mesh: row: 8 (over y, x, core), col: 4 (over z).
Axes of the slice: x: 2, y: 2, z: 4, core: 2. Of those that a mesh axis runs over, the one named last changes fastest.
Arguments:
- adjacency: float32 [1024, 32768], P('row', 'col'), may hold values from 0 to 0.99, as said below
Outputs:
- tom: float32 [1024, 1024], P('row', 'col')
Inputs may be any that keep to these rules, and one draw needn't show every extreme that they name: `adjacency`: every entry is nonnegative and below 0.99.
All inputs are finite; a program needn't handle non-finite values.
Results may differ from a plain program's by a relative error of at most 0.000059.
Values sent between devices are 32-bit elements; how exact they have to be, the bound alone decides.
No kernel may reach another device: no remote copies, remote signals or barrier semaphores. Data moves between devices by JAX's collectives and lax.ppermute only.
A program may use at most 64 MiB of HBM per device.

v0:
```python
import jax
import jax.numpy as jnp
from jax import lax
from jax.sharding import PartitionSpec as P


def inner_rows(left, right):
    return lax.dot_general(
        left,
        right,
        (((1,), (1,)), ((), ())),
        precision=lax.Precision.HIGHEST,
        preferred_element_type=jnp.float32,
    )


def finish(shared_sum, linked, own_degree, col_degree):
    smaller = jnp.minimum(own_degree[:, None], col_degree[None, :])
    return (shared_sum + linked) / (smaller + 1.0 - linked)


def degrees(adjacency, window):
    n_row = lax.axis_size("row")
    n_col = lax.axis_size("col")
    strip_rows = adjacency.shape[0]
    row_sum = jnp.sum(adjacency, axis=1)
    every = lax.all_gather(row_sum, ("row", "col"), axis=0, tiled=True)
    every = every.reshape(n_row, n_col, strip_rows).sum(axis=1).reshape(-1)
    own = lax.dynamic_slice_in_dim(every, lax.axis_index("row") * strip_rows, strip_rows, 0)
    col = lax.dynamic_slice_in_dim(every, lax.axis_index("col") * window, window, 0)
    return (own, col)


def solution(mesh):
    placed = (P("row", "col"),)
    return jax.shard_map(
        body, mesh=mesh, in_specs=placed, out_specs=P("row", "col"), check_vma=False
    )


def body(adjacency):
    strip_rows = adjacency.shape[0]
    window = strip_rows * lax.axis_size("row") // lax.axis_size("col")
    pieces = lax.all_to_all(adjacency, "row", split_axis=1, concat_axis=0, tiled=True)
    part = lax.psum_scatter(inner_rows(pieces, pieces), "row", scatter_dimension=0, tiled=True)
    shared_sum = lax.psum_scatter(part, "col", scatter_dimension=1, tiled=True)
    own_degree = lax.psum(jnp.sum(adjacency, axis=1), "col")
    all_degree = lax.all_gather(own_degree, "row", axis=0, tiled=True)
    col_degree = lax.dynamic_slice_in_dim(all_degree, lax.axis_index("col") * window, window, 0)
    linked = adjacency[:, :window]
    return finish(shared_sum, linked, own_degree, col_degree)
```

profile of v0, /device:TPU:0, one launch (start us, length us, event | category | flops | bytes accessed | tf_op | source)
XLA Modules:
  0.0 173.9 jit_solution(5790078608132117459)
XLA Ops:
  6.5 0.0 reduce-scatter.3.cloned.1.call-start
  6.5 5.6 %copy.4 = f32[128,8192]{0,1:T(8,128)} copy(f32[128,8192]{1,0:T(8,128)} %param.1) | data formatting | bytes 8388608 | tf_op args[0]
  12.1 54.3 %all_to_all.19 = f32[128,8,1024]{0,2,1:T(8,128)} all-to-all(f32[128,8,1024]{0,2,1:T(8,128)} %bitcast.8), channel_id=1, replica_groups=mesh['row'=8,'col'=4] {'row'}, dimensions={1} | all-to-all | bytes 8388608 | tf_op jit(solution)/shard_map/all_to_all | solution.py:44
  66.4 5.3 %copy.5 = f32[8,128,1024]{2,1,0:T(8,128)} copy(f32[8,128,1024]{1,2,0:T(8,128)} %bitcast.7) | data formatting | bytes 8388608 | tf_op jit(solution)/shard_map/all_to_all | solution.py:44
  71.8 18.1 %fusion = f32[1024,1024]{1,0:T(8,128)} fusion(f32[1024,1024]{1,0:T(8,128)} %bitcast.9), kind=kOutput, calls=%fused_computation.1 | convolution fusion | flops 12884901888 | bytes 8388608 | tf_op jit(solution)/shard_map/dot_general | solution.py:8
  89.9 0.0 reduce-scatter.3.cloned.1.call-update
  90.0 0.0 reduce-scatter.5.cloned.1.call-start
  90.0 51.4 %reduce-scatter.3.cloned.1.call-done = f32[128,1024]{1,0:T(8,128)} async-done(((f32[1024,1024]{1,0:T(8,128)}), f32[128,1024]{1,0:T(8,128)}) %reduce-scatter.3.cloned.1.call-update) | async-done | bytes 524304 | tf_op jit(solution)/shard_map/reduce_scatter | solution.py:45
  141.4 0.0 reduce-scatter.5.cloned.1.call-update
  141.5 2.5 %reduce_sum.9 = f32[128]{0:T(128)S(1)} reduce(f32[128,8192]{1,0:T(8,128)} %param.1, f32[]{:T(128)} %constant.6.clone.1), dimensions={1}, to_apply=%region_2.0 | reduce | flops 1048448 | bytes 4194820 | tf_op jit(solution)/shard_map/reduce_sum | solution.py:47
  144.0 11.8 %psum.7 = f32[128]{0:T(128)S(1)} all-reduce(f32[128]{0:T(128)S(1)} %reduce_sum.9), channel_id=1, replica_groups=mesh['row'=8,'col'=4] {'col'}, use_global_device_ids=true, to_apply=%region_3.0 | all-reduce | flops 128 | bytes 1024 | tf_op jit(solution)/shard_map/psum | solution.py:47
  155.7 8.6 %all-gather = f32[8,1,128]{2,1,0:T(1,128)S(1)} all-gather(f32[1,1,128]{2,1,0:T(1,128)S(1)} %bitcast.11), channel_id=1, replica_groups=mesh['row'=8,'col'=4] {'row'}, dimensions={0}, use_global_device_ids=true | all-gather | bytes 4608 | tf_op jit(solution)/shard_map/all_gather | solution.py:48
  164.3 0.1 dynamic_slice.3
  164.4 1.0 reduce-scatter.5.cloned.1.call-done
  165.3 1.7 subtract_divide_fusion
Async XLA Ops:
  6.5 134.9 %reduce-scatter.3.cloned.1.call-start = ((), (), s32[]{:S(2)}) async-start(), calls=%async_computation.3 | async-start | bytes 4718592 | tf_op jit(solution)/shard_map/reduce_scatter | solution.py:45
  90.0 75.4 %reduce-scatter.5.cloned.1.call-start = ((), (), s32[]{:S(2)}) async-start(), calls=%async_computation.4 | async-start | bytes 655360 | tf_op jit(solution)/shard_map/reduce_scatter | solution.py:46
Sparse Core Ops, SparseCore 0:
  90.1 51.3 reduce-scatter.2
  143.8 21.4 reduce-scatter.4
where the time goes:
time: 174 us
  blocking collectives  74.7 us (43%)
  waiting for transfers between devices  52.4 us (30%)
  matrix products  18.1 us (10%)
  between operations  13.4 us (8%)
  local copies, waits for them, and re-layouts  11 us (6%)
  other arithmetic  4.22 us (2%)
    all_to_all x1, blocking collectives, body(): lax.all_to_all(adjacency, 'row', split_axis=1, concat_axis=0, tiled=True)  54.3 us
    reduce_scatter x1, waiting for transfers between devices, body(): lax.psum_scatter(inner_rows(pieces, pieces), 'row', scatter_dimension=0,...  51.4 us
    dot_general x1, matrix products, inner_rows(): lax.dot_general(left, right, (((1,), (1,)), ((), ())), precision=lax.Prec...  18.1 us
    psum x1, blocking collectives, body(): own_degree = lax.psum(jnp.sum(adjacency, axis=1), 'col')  11.8 us
    all_gather x1, blocking collectives, body(): all_degree = lax.all_gather(own_degree, 'row', axis=0, tiled=True)  8.59 us
    unnamed x1, local copies, waits for them, and re-layouts  5.57 us
    all_to_all x1, local copies, waits for them, and re-layouts, body(): lax.all_to_all(adjacency, 'row', split_axis=1, concat_axis=0, tiled=True)  5.34 us
  transfers between devices with their start and end apart: 2, of which 2 were waited for; matrix products, arithmetic and copies ran while one was open for 1% of the time, Pallas kernels for 0%

commit v1 on v0

--- a/solution.py
+++ b/solution.py
@@ -41,7 +41,10 @@
 def body(adjacency):
     strip_rows = adjacency.shape[0]
     window = strip_rows * lax.axis_size("row") // lax.axis_size("col")
-    pieces = lax.all_to_all(adjacency, "row", split_axis=1, concat_axis=0, tiled=True)
+    pieces = jnp.concatenate(
+        lax.all_to_all(jnp.stack(jnp.split(adjacency, lax.axis_size("row"), axis=1)), "row", 0, 0),
+        axis=0,
+    )
     part = lax.psum_scatter(inner_rows(pieces, pieces), "row", scatter_dimension=0, tiled=True)
     shared_sum = lax.psum_scatter(part, "col", scatter_dimension=1, tiled=True)
     own_degree = lax.psum(jnp.sum(adjacency, axis=1), "col")

time: 174 us -> 168 us (0.966)
  matrix products: 18.1 us -> 14.8 us
  local copies, waits for them, and re-layouts: 11 us -> 8.71 us
    all_to_all x1 -> x0, local copies, waits for them, and re-layouts: 5.34 us -> none  [body(): lax.all_to_all(adjacency, 'row', split_axis=1, concat_axis=0, tiled=True)]
    dot_general x1, matrix products: 18.1 us -> 14.8 us  [inner_rows(): lax.dot_general(left, right, (((1,), (1,)), ((), ())), precision=lax.Prec...]
    unnamed x1 -> x7, local copies, waits for them, and re-layouts: 5.57 us -> 7.56 us
  transfers between devices with their start and end apart: 2 -> 2, of which waited for: 2 -> 2; matrix products, arithmetic and copies ran while one was open for 1% -> 2% of each run, Pallas kernels for 0% -> 0%
where the time goes in v1:
time: 168 us; the launch traced here: 167 us
  blocking collectives  74.4 us (44%)
  waiting for transfers between devices  51.8 us (31%)
  matrix products  14.8 us (9%)
  between operations  13.4 us (8%)
  local copies, waits for them, and re-layouts  8.71 us (5%)
  other arithmetic  4.22 us (3%)
    all_to_all x1, blocking collectives, body(): lax.all_to_all(jnp.stack(jnp.split(adjacency, lax.axis_size('row'), axis=...  54 us
    reduce_scatter x1, waiting for transfers between devices, body(): lax.psum_scatter(inner_rows(pieces, pieces), 'row', scatter_dimension=0,...  50.8 us
    dot_general x1, matrix products, inner_rows(): lax.dot_general(left, right, (((1,), (1,)), ((), ())), precision=lax.Prec...  14.8 us
    psum x1, blocking collectives, body(): own_degree = lax.psum(jnp.sum(adjacency, axis=1), 'col')  11.8 us
    all_gather x1, blocking collectives, body(): all_degree = lax.all_gather(own_degree, 'row', axis=0, tiled=True)  8.61 us
    unnamed x7, local copies, waits for them, and re-layouts  7.56 us
  transfers between devices with their start and end apart: 2, of which 2 were waited for; matrix products, arithmetic and copies ran while one was open for 2% of the time, Pallas kernels for 0%

profile of v1, /device:TPU:0, one launch (start us, length us, event | category | flops | bytes accessed | tf_op | source)
XLA Modules:
  0.0 167.4 jit_solution(14416462727775434973)
XLA Ops:
  6.5 0.0 reduce-scatter.3.cloned.1.call-start
  6.5 1.1 bitcast_dynamic-update-slice_fusion.7
  7.6 1.1 bitcast_dynamic-update-slice_fusion.6
  8.7 1.1 bitcast_dynamic-update-slice_fusion.5
  9.8 1.1 bitcast_dynamic-update-slice_fusion.4
  10.9 1.1 bitcast_dynamic-update-slice_fusion.3
  12.0 1.1 bitcast_dynamic-update-slice_fusion.2
  13.0 1.1 bitcast_dynamic-update-slice_fusion.1
  14.1 1.1 bitcast_dynamic-update-slice_fusion
  15.2 54.0 %all_to_all.5 = f32[8,128,1024]{2,1,0:T(8,128)S(1)} all-to-all(f32[8,128,1024]{2,1,0:T(8,128)S(1)} %bitcast_dynamic-update-slice_fusion), channel_id=1, replica_groups=mesh['row'=8,'col'=4] {'row'}, dimensions={0} | all-to-all | bytes 8388608 | tf_op jit(solution)/shard_map/all_to_all | solution.py:45
  69.2 14.8 %fusion = f32[1024,1024]{1,0:T(8,128)} fusion(f32[1024,1024]{1,0:T(8,128)S(1)} %bitcast.21), kind=kOutput, calls=%fused_computation.9 | convolution fusion | flops 12884901888 | bytes 8388608 | tf_op jit(solution)/shard_map/dot_general | solution.py:8
  84.0 0.0 reduce-scatter.3.cloned.1.call-update
  84.0 0.0 reduce-scatter.5.cloned.1.call-start
  84.1 50.8 %reduce-scatter.3.cloned.1.call-done = f32[128,1024]{1,0:T(8,128)} async-done(((f32[1024,1024]{1,0:T(8,128)}), f32[128,1024]{1,0:T(8,128)}) %reduce-scatter.3.cloned.1.call-update) | async-done | bytes 524304 | tf_op jit(solution)/shard_map/reduce_scatter | solution.py:48
  134.9 0.0 reduce-scatter.5.cloned.1.call-update
  134.9 2.5 %reduce_sum.9 = f32[128]{0:T(128)S(1)} reduce(f32[128,8192]{1,0:T(8,128)} %param.1, f32[]{:T(128)} %constant.6.clone.1), dimensions={1}, to_apply=%region_2.0 | reduce | flops 1048448 | bytes 4194820 | tf_op jit(solution)/shard_map/reduce_sum | solution.py:50
  137.4 11.8 %psum.7 = f32[128]{0:T(128)S(1)} all-reduce(f32[128]{0:T(128)S(1)} %reduce_sum.9), channel_id=1, replica_groups=mesh['row'=8,'col'=4] {'col'}, use_global_device_ids=true, to_apply=%region_3.0 | all-reduce | flops 128 | bytes 1024 | tf_op jit(solution)/shard_map/psum | solution.py:50
  149.2 8.6 %all-gather = f32[8,1,128]{2,1,0:T(1,128)S(1)} all-gather(f32[1,1,128]{2,1,0:T(1,128)S(1)} %bitcast.23), channel_id=1, replica_groups=mesh['row'=8,'col'=4] {'row'}, dimensions={0}, use_global_device_ids=true | all-gather | bytes 4608 | tf_op jit(solution)/shard_map/all_gather | solution.py:51
  157.8 0.1 dynamic_slice.3
  157.8 1.0 reduce-scatter.5.cloned.1.call-done
  158.8 1.7 %subtract_divide_fusion = f32[128,256]{1,0:T(8,128)} fusion(f32[128,256]{1,0:T(8,128)} %reduce-scatter.5.cloned.1.call-done, f32[128,8192]{1,0:T(8,128)} %param.1, f32[256]{0:T(256)S(1)} %dynamic_slice.3, f32[128]{0:T(128)S(1)} %psum.7), kind=kLoop, calls=%fused_computation.8 | loop fusion | flops 163840 | bytes 394752 | tf_op jit(solution)/shard_map/div | solution.py:19
Async XLA Ops:
  6.5 128.3 %reduce-scatter.3.cloned.1.call-start = ((), (), s32[]{:S(2)}) async-start(), calls=%async_computation.3 | async-start | bytes 4718592 | tf_op jit(solution)/shard_map/reduce_scatter | solution.py:48
  84.0 74.8 %reduce-scatter.5.cloned.1.call-start = ((), (), s32[]{:S(2)}) async-start(), calls=%async_computation.4 | async-start | bytes 655360 | tf_op jit(solution)/shard_map/reduce_scatter | solution.py:49
Sparse Core Ops, SparseCore 0:
  84.1 50.6 reduce-scatter.2
  137.2 21.5 reduce-scatter.4

commit v2 on v0

--- a/solution.py
+++ b/solution.py
@@ -45,7 +45,12 @@
     part = lax.psum_scatter(inner_rows(pieces, pieces), "row", scatter_dimension=0, tiled=True)
     shared_sum = lax.psum_scatter(part, "col", scatter_dimension=1, tiled=True)
     own_degree = lax.psum(jnp.sum(adjacency, axis=1), "col")
-    all_degree = lax.all_gather(own_degree, "row", axis=0, tiled=True)
+    ring = [own_degree]
+    for hop in range(7):
+        ring.append(lax.ppermute(ring[-1], "row", [(dev, (dev + 1) % 8) for dev in range(8)]))
+    all_degree = jnp.roll(
+        jnp.concatenate(ring[::-1], axis=0), (lax.axis_index("row") + 1) * ring[0].shape[0], axis=0
+    )
     col_degree = lax.dynamic_slice_in_dim(all_degree, lax.axis_index("col") * window, window, 0)
     linked = adjacency[:, :window]
     return finish(shared_sum, linked, own_degree, col_degree)

time: 174 us -> 174 us (level)
  blocking collectives: 74.7 us -> 66.9 us
  waiting for transfers between devices: 52.4 us -> 60.1 us
    reduce_scatter x1, waiting for transfers between devices: 51.4 us -> 9.2 us  [body(): lax.psum_scatter(inner_rows(pieces, pieces), 'row', scatter_dimension=0,...]
    ppermute x0 -> x7, waiting for transfers between devices: none -> 27 us  [body(): lax.ppermute(ring[-1], 'row', [(dev, (dev + 1) % 8) for dev in range(8)])]
    reduce_scatter x1, waiting for transfers between devices: 0.96 us -> 23.8 us  [body(): shared_sum = lax.psum_scatter(part, 'col', scatter_dimension=1, tiled=True)]
    all_gather x1 -> x0, blocking collectives: 8.59 us -> none  [body(): all_degree = lax.all_gather(own_degree, 'row', axis=0, tiled=True)]
    unnamed x1 -> x16, local copies, waits for them, and re-layouts: 5.57 us -> 5.66 us
  transfers between devices with their start and end apart: 2 -> 9, of which waited for: 2 -> 9; matrix products, arithmetic and copies ran while one was open for 1% -> 2% of each run, Pallas kernels for 0% -> 0%
where the time goes in v2:
time: 174 us
  blocking collectives  66.9 us (38%)
  waiting for transfers between devices  60.1 us (35%)
  matrix products  18.1 us (10%)
  between operations  13.5 us (8%)
  local copies, waits for them, and re-layouts  11.1 us (6%)
  other arithmetic  4.22 us (2%)
    all_to_all x1, blocking collectives, body(): lax.all_to_all(adjacency, 'row', split_axis=1, concat_axis=0, tiled=True)  54.3 us
    ppermute x7, waiting for transfers between devices, body(): lax.ppermute(ring[-1], 'row', [(dev, (dev + 1) % 8) for dev in range(8)])  27 us
    reduce_scatter x1, waiting for transfers between devices, body(): shared_sum = lax.psum_scatter(part, 'col', scatter_dimension=1, tiled=True)  23.8 us
    dot_general x1, matrix products, inner_rows(): lax.dot_general(left, right, (((1,), (1,)), ((), ())), precision=lax.Prec...  18.1 us
    psum x1, blocking collectives, body(): own_degree = lax.psum(jnp.sum(adjacency, axis=1), 'col')  12.6 us
    reduce_scatter x1, waiting for transfers between devices, body(): lax.psum_scatter(inner_rows(pieces, pieces), 'row', scatter_dimension=0,...  9.2 us
    unnamed x16, local copies, waits for them, and re-layouts  5.66 us
    all_to_all x1, local copies, waits for them, and re-layouts, body(): lax.all_to_all(adjacency, 'row', split_axis=1, concat_axis=0, tiled=True)  5.35 us
  transfers between devices with their start and end apart: 9, of which 9 were waited for; matrix products, arithmetic and copies ran while one was open for 2% of the time, Pallas kernels for 0%

profile of v2, /device:TPU:0, one launch (start us, length us, event | category | flops | bytes accessed | tf_op | source)
XLA Modules:
  0.0 174.1 jit_solution(9203494418040893911)
XLA Ops:
  6.5 0.0 reduce-scatter.3.cloned.1.call-start
  6.5 5.6 %copy.2 = f32[128,8192]{0,1:T(8,128)} copy(f32[128,8192]{1,0:T(8,128)} %param.1) | data formatting | bytes 8388608 | tf_op args[0]
  12.1 54.3 %all_to_all.19 = f32[128,8,1024]{0,2,1:T(8,128)} all-to-all(f32[128,8,1024]{0,2,1:T(8,128)} %bitcast.6), channel_id=1, replica_groups=mesh['row'=8,'col'=4] {'row'}, dimensions={1} | all-to-all | bytes 8388608 | tf_op jit(solution)/shard_map/all_to_all | solution.py:44
  66.4 5.4 %copy.3 = f32[8,128,1024]{2,1,0:T(8,128)} copy(f32[8,128,1024]{1,2,0:T(8,128)} %bitcast.5) | data formatting | bytes 8388608 | tf_op jit(solution)/shard_map/all_to_all | solution.py:44
  71.8 18.1 %fusion = f32[1024,1024]{1,0:T(8,128)} fusion(f32[1024,1024]{1,0:T(8,128)} %bitcast.7), kind=kOutput, calls=%fused_computation.17 | convolution fusion | flops 12884901888 | bytes 8388608 | tf_op jit(solution)/shard_map/dot_general | solution.py:8
  89.9 0.0 reduce-scatter.3.cloned.1.call-update
  90.0 0.0 reduce-scatter.5.cloned.1.call-start
  90.0 2.5 %reduce_sum.9 = f32[128]{0:T(128)S(1)} reduce(f32[128,8192]{1,0:T(8,128)} %param.1, f32[]{:T(128)} %constant.35.clone.1), dimensions={1}, to_apply=%region_2.0 | reduce | flops 1048448 | bytes 4194820 | tf_op jit(solution)/shard_map/reduce_sum | solution.py:47
  92.5 12.6 %psum.7 = f32[128]{0:T(128)S(1)} all-reduce(f32[128]{0:T(128)S(1)} %reduce_sum.9), channel_id=1, replica_groups=mesh['row'=8,'col'=4] {'col'}, use_global_device_ids=true, to_apply=%region_3.0 | all-reduce | flops 128 | bytes 1024 | tf_op jit(solution)/shard_map/psum | solution.py:47
  105.1 0.0 collective-permute-start
  105.1 3.9 %collective-permute-done = f32[128]{0:T(128)S(1)} collective-permute-done((f32[128]{0:T(128)S(1)}, f32[128]{0:T(128)S(1)}, u32[]{:S(2)}, u32[]{:S(2)}) %collective-permute-start) | collective-permute-done | bytes 544 | tf_op jit(solution)/shard_map/ppermute | solution.py:50
  109.0 0.0 collective-permute-start.1
  109.0 3.9 %collective-permute-done.1 = f32[128]{0:T(128)S(1)} collective-permute-done((f32[128]{0:T(128)S(1)}, f32[128]{0:T(128)S(1)}, u32[]{:S(2)}, u32[]{:S(2)}) %collective-permute-start.1) | collective-permute-done | bytes 544 | tf_op jit(solution)/shard_map/ppermute | solution.py:50
  112.9 0.0 collective-permute-start.2
  112.9 3.9 %collective-permute-done.2 = f32[128]{0:T(128)S(1)} collective-permute-done((f32[128]{0:T(128)S(1)}, f32[128]{0:T(128)S(1)}, u32[]{:S(2)}, u32[]{:S(2)}) %collective-permute-start.2) | collective-permute-done | bytes 544 | tf_op jit(solution)/shard_map/ppermute | solution.py:50
  116.7 0.0 collective-permute-start.3
  116.7 3.9 %collective-permute-done.3 = f32[128]{0:T(128)S(1)} collective-permute-done((f32[128]{0:T(128)S(1)}, f32[128]{0:T(128)S(1)}, u32[]{:S(2)}, u32[]{:S(2)}) %collective-permute-start.3) | collective-permute-done | bytes 544 | tf_op jit(solution)/shard_map/ppermute | solution.py:50
  120.6 0.0 collective-permute-start.4
  120.6 3.9 %collective-permute-done.4 = f32[128]{0:T(128)S(1)} collective-permute-done((f32[128]{0:T(128)S(1)}, f32[128]{0:T(128)S(1)}, u32[]{:S(2)}, u32[]{:S(2)}) %collective-permute-start.4) | collective-permute-done | bytes 544 | tf_op jit(solution)/shard_map/ppermute | solution.py:50
  124.5 0.0 collective-permute-start.5
  124.5 3.9 %collective-permute-done.5 = f32[128]{0:T(128)S(1)} collective-permute-done((f32[128]{0:T(128)S(1)}, f32[128]{0:T(128)S(1)}, u32[]{:S(2)}, u32[]{:S(2)}) %collective-permute-start.5) | collective-permute-done | bytes 544 | tf_op jit(solution)/shard_map/ppermute | solution.py:50
  128.3 0.0 collective-permute-start.6
  128.3 3.9 %collective-permute-done.6 = f32[128]{0:T(128)S(1)} collective-permute-done((f32[128]{0:T(128)S(1)}, f32[128]{0:T(128)S(1)}, u32[]{:S(2)}, u32[]{:S(2)}) %collective-permute-start.6) | collective-permute-done | bytes 544 | tf_op jit(solution)/shard_map/ppermute | solution.py:50
  132.3 9.2 %reduce-scatter.3.cloned.1.call-done = f32[128,1024]{1,0:T(8,128)} async-done(((f32[1024,1024]{1,0:T(8,128)}), f32[128,1024]{1,0:T(8,128)}) %reduce-scatter.3.cloned.1.call-update) | async-done | bytes 524304 | tf_op jit(solution)/shard_map/reduce_scatter | solution.py:45
  141.5 0.0 reduce-scatter.5.cloned.1.call-update
  141.6 0.1 dynamic_slice.8
  141.7 23.8 %reduce-scatter.5.cloned.1.call-done = f32[128,256]{1,0:T(8,128)} async-done(((f32[128,1024]{1,0:T(8,128)}), f32[128,256]{1,0:T(8,128)}) %reduce-scatter.5.cloned.1.call-update) | async-done | bytes 131088 | tf_op jit(solution)/shard_map/reduce_scatter | solution.py:46
  165.5 1.7 subtract_divide_fusion
  (17 shorter events, 0.1 us)
Async XLA Ops:
  6.5 134.9 %reduce-scatter.3.cloned.1.call-start = ((), (), s32[]{:S(2)}) async-start(), calls=%async_computation.3 | async-start | bytes 4718592 | tf_op jit(solution)/shard_map/reduce_scatter | solution.py:45
  90.0 75.6 %reduce-scatter.5.cloned.1.call-start = ((), (), s32[]{:S(2)}) async-start(), calls=%async_computation.4 | async-start | bytes 655360 | tf_op jit(solution)/shard_map/reduce_scatter | solution.py:46
  105.1 3.9 %collective-permute-start = (f32[128]{0:T(128)S(1)}, f32[128]{0:T(128)S(1)}, u32[]{:S(2)}, u32[]{:S(2)}) collective-permute-start(f32[128]{0:T(128)S(1)} %psum.7), channel_id=1, source_target_pairs={{0,4},{4,8},{8,12},{12,16},{16,20},{20,24},{24,28},{28,0},{1,5},{5... | collective-permute-start | bytes 1544 | tf_op jit(solution)/shard_map/ppermute | solution.py:50
  109.0 3.9 %collective-permute-start.1 = (f32[128]{0:T(128)S(1)}, f32[128]{0:T(128)S(1)}, u32[]{:S(2)}, u32[]{:S(2)}) collective-permute-start(f32[128]{0:T(128)S(1)} %collective-permute-done), channel_id=1, source_target_pairs={{0,4},{4,8},{8,12},{12,16},{16,20},{20,24},{24,28},{28,0},{1,5},{5... | collective-permute-start | bytes 1544 | tf_op jit(solution)/shard_map/ppermute | solution.py:50
  112.9 3.9 %collective-permute-start.2 = (f32[128]{0:T(128)S(1)}, f32[128]{0:T(128)S(1)}, u32[]{:S(2)}, u32[]{:S(2)}) collective-permute-start(f32[128]{0:T(128)S(1)} %collective-permute-done.1), channel_id=1, source_target_pairs={{0,4},{4,8},{8,12},{12,16},{16,20},{20,24},{24,28},{28,0},{1,5},{5... | collective-permute-start | bytes 1544 | tf_op jit(solution)/shard_map/ppermute | solution.py:50
  116.7 3.9 %collective-permute-start.3 = (f32[128]{0:T(128)S(1)}, f32[128]{0:T(128)S(1)}, u32[]{:S(2)}, u32[]{:S(2)}) collective-permute-start(f32[128]{0:T(128)S(1)} %collective-permute-done.2), channel_id=1, source_target_pairs={{0,4},{4,8},{8,12},{12,16},{16,20},{20,24},{24,28},{28,0},{1,5},{5... | collective-permute-start | bytes 1544 | tf_op jit(solution)/shard_map/ppermute | solution.py:50
  120.6 3.9 %collective-permute-start.4 = (f32[128]{0:T(128)S(1)}, f32[128]{0:T(128)S(1)}, u32[]{:S(2)}, u32[]{:S(2)}) collective-permute-start(f32[128]{0:T(128)S(1)} %collective-permute-done.3), channel_id=1, source_target_pairs={{0,4},{4,8},{8,12},{12,16},{16,20},{20,24},{24,28},{28,0},{1,5},{5... | collective-permute-start | bytes 1544 | tf_op jit(solution)/shard_map/ppermute | solution.py:50
  124.5 3.9 %collective-permute-start.5 = (f32[128]{0:T(128)S(1)}, f32[128]{0:T(128)S(1)}, u32[]{:S(2)}, u32[]{:S(2)}) collective-permute-start(f32[128]{0:T(128)S(1)} %collective-permute-done.4), channel_id=1, source_target_pairs={{0,4},{4,8},{8,12},{12,16},{16,20},{20,24},{24,28},{28,0},{1,5},{5... | collective-permute-start | bytes 1544 | tf_op jit(solution)/shard_map/ppermute | solution.py:50
  128.3 3.9 %collective-permute-start.6 = (f32[128]{0:T(128)S(1)}, f32[128]{0:T(128)S(1)}, u32[]{:S(2)}, u32[]{:S(2)}) collective-permute-start(f32[128]{0:T(128)S(1)} %collective-permute-done.5), channel_id=1, source_target_pairs={{0,4},{4,8},{8,12},{12,16},{16,20},{20,24},{24,28},{28,0},{1,5},{5... | collective-permute-start | bytes 1544 | tf_op jit(solution)/shard_map/ppermute | solution.py:50
Sparse Core Ops, SparseCore 0:
  90.1 51.3 reduce-scatter.2
  143.8 21.6 reduce-scatter.4
